TPU v7x, 32 devices: a whole 2x2x4 slice. The times are simulated.
32 devices in a mesh: row: 8 (over y, x, core), col: 4 (over z).
Axes of the slice: x: 2, y: 2, z: 4, core: 2. Of those that a mesh axis runs over, the one named last changes fastest.
Arguments:
- out_grads: bfloat16 [64, 28672], P('col', 'row'), may hold values from -6 to 6
- in_acts: bfloat16 [64, 8192], P('row', 'col'), may hold values from -6 to 6
- out_basis: bfloat16 [28672, 28672], P('row', 'col'), may hold values from -0.03125 to 0.03125
- in_basis: bfloat16 [8192, 8192], P('col', 'row'), may hold values from -0.0625 to 0.0625
- eigenvalues: bfloat16 [28672, 8192], P('col', 'row'), may hold values from 0.019897461 to 2
- queries: bfloat16 [2, 28672, 8192], P(None, 'col', 'row'), may hold values from -0.00015640259 to 0.00015640259
Outputs:
- scores: float32 [2, 64], replicated
All inputs are finite; a program needn't handle non-finite values.
Results may differ from a plain program's by a relative error of at most 0.0045.
Values may be sent and summed in bfloat16 or wider, within the bound.
No kernel may reach another device: no remote copies, remote signals or barrier semaphores. Data moves between devices by JAX's collectives and lax.ppermute only.
A program may use at most 192 MiB of HBM per device.

v0:
```python
import jax
import jax.numpy as jnp
from jax import lax
from jax.sharding import PartitionSpec as P

DAMPING = 0.1


def local(out_grads, in_acts, out_basis, in_basis, eigenvalues, queries):
    grads_all = lax.all_gather(out_grads, "col", axis=0, tiled=True)
    grad_mine = lax.psum_scatter(
        jnp.dot(grads_all, out_basis, preferred_element_type=jnp.float32),
        "row",
        scatter_dimension=0,
        tiled=True,
    ).astype(jnp.bfloat16)
    grad_rot = lax.all_gather(grad_mine, "row", axis=0, tiled=True)
    acts_all = lax.all_gather(in_acts, "row", axis=0, tiled=True)
    act_part = jnp.dot(acts_all, in_basis, preferred_element_type=jnp.float32)
    act_rot = lax.psum(act_part, "col").astype(jnp.bfloat16)
    shifted = eigenvalues.astype(jnp.float32) + DAMPING
    scaled = queries.astype(jnp.float32) / shifted[None]
    lifted = jnp.einsum(
        "qkj,tj->qkt",
        scaled,
        act_rot.astype(jnp.float32),
        precision=lax.Precision.HIGHEST,
        preferred_element_type=jnp.float32,
    )
    partial_scores = jnp.einsum(
        "qkt,tk->qt", lifted, grad_rot.astype(jnp.float32), precision=lax.Precision.HIGHEST
    )
    return lax.psum(partial_scores, ("row", "col"))


def solution(mesh):
    in_specs = (
        P("col", "row"),
        P("row", "col"),
        P("row", "col"),
        P("col", "row"),
        P("col", "row"),
        P(None, "col", "row"),
    )
    out_specs = P()
    return jax.shard_map(local, mesh=mesh, in_specs=in_specs, out_specs=out_specs, check_vma=False)
```

profile of v0, /device:TPU:0, one launch (start us, length us, event | category | flops | bytes accessed | tf_op | source)
XLA Modules:
  0.0 220.7 jit_solution(7782558009660924071)
XLA Ops:
  6.5 0.0 reduce-scatter.2.cloned.1.call-start
  6.5 17.0 %all_gather.9 = bf16[64,3584]{1,0:T(8,128)(2,1)S(1)} all-gather(bf16[16,3584]{1,0:T(8,128)(2,1)} %param.6), channel_id=1, replica_groups=mesh['row'=8,'col'=4] {'col'}, dimensions={0}, use_global_device_ids=true | all-gather | bytes 573440 | tf_op jit(solution)/shard_map/all_gather | solution.py:10
  23.5 21.8 %fusion.7 = f32[64,7168]{1,0:T(8,128)} fusion(bf16[64,3584]{1,0:T(8,128)(2,1)S(1)} %all_gather.9, bf16[3584,7168]{1,0:T(8,128)(2,1)} %param.8), kind=kOutput, calls=%fused_computation.9 | convolution fusion | flops 3288334336 | bytes 53673984 | tf_op jit(solution)/shard_map/dot_general | solution.py:12
  45.3 0.0 copy-start.1
  45.3 0.0 reduce-scatter.2.cloned.1.call-update
  45.4 0.0 copy-start
  45.4 17.4 %convert_add_fusion = f32[7168,1024]{1,0:T(8,128)} fusion(bf16[7168,1024]{1,0:T(8,128)(2,1)} %param.10), kind=kLoop, calls=%fused_computation.3 | loop fusion | flops 14680064 | bytes 44040192 | tf_op jit(solution)/shard_map/add | solution.py:21
  62.8 0.0 copy-done.1
  62.8 9.4 %all_gather.11 = bf16[64,2048]{1,0:T(8,128)(2,1)S(1)} all-gather(bf16[8,2048]{1,0:T(8,128)(2,1)S(1)} %copy-done.1), channel_id=1, replica_groups=mesh['row'=8,'col'=4] {'row'}, dimensions={0}, use_global_device_ids=true | all-gather | bytes 294912 | tf_op jit(solution)/shard_map/all_gather | solution.py:18
  72.2 0.0 copy-done
  72.2 0.8 fusion.8
  73.1 25.6 %all-reduce.1 = bf16[64,1024]{1,0:T(8,128)(2,1)S(1)} all-reduce(f32[64,1024]{1,0:T(8,128)S(1)} %fusion.8), channel_id=1, replica_groups=mesh['row'=8,'col'=4] {'col'}, use_global_device_ids=true, to_apply=%region_1.0 | all-reduce | flops 65536 | bytes 393216 | tf_op jit(solution)/shard_map/psum | solution.py:20
  98.7 45.4 %fusion = f32[2,7168,64]{1,2,0:T(8,128)} fusion(bf16[2,7168,1024]{2,1,0:T(8,128)(2,1)} %param.11, f32[7168,1024]{1,0:T(8,128)} %convert_add_fusion, bf16[64,1024]{1,0:T(8,128)(2,1)S(1)} %all-reduce.1), kind=kOutput, calls=%fused_computation.1 | convolution fusion | flops 11303649280 | bytes 62521344 | tf_op jit(solution)/shard_map/qkj,tj->qkt/dot_general | solution.py:23
  144.1 0.0 reduce-scatter.2.cloned.1.call-done
  144.1 1.0 convert_element_type.14
  145.1 11.0 %all_gather.10 = bf16[64,7168]{1,0:T(8,128)(2,1)S(1)} all-gather(bf16[8,7168]{1,0:T(8,128)(2,1)S(1)} %convert_element_type.14), channel_id=1, replica_groups=mesh['row'=8,'col'=4] {'row'}, dimensions={0}, use_global_device_ids=true | all-gather | bytes 1032192 | tf_op jit(solution)/shard_map/all_gather | solution.py:17
  156.0 19.9 %fusion.2 = f32[64,1,2]{2,1,0:T(1,128)S(1)} fusion(f32[2,7168,64]{1,2,0:T(8,128)} %fusion, bf16[64,7168,1]{1,0,2:T(8,128)(2,1)S(1)} %bitcast.11), kind=kOutput, calls=%fused_computation.4 | convolution fusion | flops 11010048 | bytes 4588032 | tf_op jit(solution)/shard_map/qkt,tk->qt/dot_general | solution.py:30
  175.9 0.1 copy.9
  176.0 37.8 %psum.15 = f32[2,64]{1,0:T(2,128)} all-reduce(f32[2,64]{1,0:T(2,128)S(1)} %bitcast.12), channel_id=1, replica_groups=mesh['row'=8,'col'=4] {'row','col'}, use_global_device_ids=true, to_apply=%region_2.0 | all-reduce | flops 128 | bytes 1024 | tf_op jit(solution)/shard_map/psum | solution.py:33
Async XLA Ops:
  6.5 137.6 %reduce-scatter.2.cloned.1.call-start = ((), (), s32[]{:S(2)}) async-start(), calls=%async_computation.1 | async-start | bytes 2064384 | tf_op jit(solution)/shard_map/reduce_scatter | solution.py:11
  45.3 17.4 %copy-start.1 = (bf16[8,2048]{1,0:T(8,128)(2,1)S(1)}, bf16[8,2048]{1,0:T(8,128)(2,1)}, u32[]{:S(2)}) copy-start(bf16[8,2048]{1,0:T(8,128)(2,1)} %param.7) | copy-start | bytes 98308
  45.4 26.8 %copy-start = (bf16[2048,1024]{1,0:T(8,128)(2,1)S(1)}, bf16[2048,1024]{1,0:T(8,128)(2,1)}, u32[]{:S(2)}) copy-start(bf16[2048,1024]{1,0:T(8,128)(2,1)} %param.9) | copy-start | bytes 12582916
Sparse Core Ops, SparseCore 0:
  45.5 42.0 reduce-scatter.1
where the time goes:
time: 221 us
  blocking collectives  101 us (46%)
  matrix products  88 us (40%)
  other arithmetic  18.3 us (8%)
  between operations  13.4 us (6%)
    dot_general x1, matrix products, local(): jnp.einsum('qkj,tj->qkt', scaled, act_rot.astype(jnp.float32), precision=...  45.4 us
    psum x1, blocking collectives, local(): return lax.psum(partial_scores, ('row', 'col'))  37.8 us
    psum x1, blocking collectives, local(): act_rot = lax.psum(act_part, 'col').astype(jnp.bfloat16)  25.6 us
    dot_general x1, matrix products, local(): jnp.dot(grads_all, out_basis, preferred_element_type=jnp.float32)  21.8 us
    dot_general x1, matrix products, local(): jnp.einsum('qkt,tk->qt', lifted, grad_rot.astype(jnp.float32), precision=...  19.9 us
    add x1, other arithmetic, local(): shifted = eigenvalues.astype(jnp.float32) + DAMPING  17.4 us
    all_gather x1, blocking collectives, local(): grads_all = lax.all_gather(out_grads, 'col', axis=0, tiled=True)  17 us
    all_gather x1, blocking collectives, local(): grad_rot = lax.all_gather(grad_mine, 'row', axis=0, tiled=True)  11 us
  transfers between devices with their start and end apart: 1, of which 0 were waited for; matrix products, arithmetic and copies ran while one was open for 29% of the time, Pallas kernels for 0%

commit v1 on v0

--- a/solution.py
+++ b/solution.py
@@ -4,6 +4,11 @@
 from jax.sharding import PartitionSpec as P
 
 DAMPING = 0.1
+
+
+def summed_here(x, axis):
+    blocks = lax.all_gather(x, axis)
+    return jnp.sum(blocks, axis=0)
 
 
 def local(out_grads, in_acts, out_basis, in_basis, eigenvalues, queries):
@@ -17,7 +22,7 @@
     grad_rot = lax.all_gather(grad_mine, "row", axis=0, tiled=True)
     acts_all = lax.all_gather(in_acts, "row", axis=0, tiled=True)
     act_part = jnp.dot(acts_all, in_basis, preferred_element_type=jnp.float32)
-    act_rot = lax.psum(act_part, "col").astype(jnp.bfloat16)
+    act_rot = summed_here(act_part, "col").astype(jnp.bfloat16)
     shifted = eigenvalues.astype(jnp.float32) + DAMPING
     scaled = queries.astype(jnp.float32) / shifted[None]
     lifted = jnp.einsum(

time: 221 us -> 205 us (0.928)
  blocking collectives: 101 us -> 79.3 us
  matrix products: 88 us -> 91.1 us
    psum x1 -> x0, blocking collectives: 25.6 us -> none  [local(): act_rot = lax.psum(act_part, 'col').astype(jnp.bfloat16)]
    all_gather x1, blocking collectives: 17 us -> 20 us  [local(): grads_all = lax.all_gather(out_grads, 'col', axis=0, tiled=True)]
    dot_general x1, matrix products: 0.85 us -> 3.72 us  [local(): act_part = jnp.dot(acts_all, in_basis, preferred_element_type=jnp.float32)]
  transfers between devices with their start and end apart: 1 -> 2, of which waited for: 0 -> 0; matrix products, arithmetic and copies ran while one was open for 29% -> 42% of each run, Pallas kernels for 0% -> 0%
where the time goes in v1:
time: 205 us
  matrix products  91.1 us (44%)
  blocking collectives  79.3 us (39%)
  other arithmetic  19.2 us (9%)
  between operations  14.8 us (7%)
    dot_general x1, matrix products, local(): jnp.einsum('qkj,tj->qkt', scaled, act_rot.astype(jnp.float32), precision=...  45.7 us
    psum x1, blocking collectives, local(): return lax.psum(partial_scores, ('row', 'col'))  37.9 us
    dot_general x1, matrix products, local(): jnp.dot(grads_all, out_basis, preferred_element_type=jnp.float32)  21.8 us
    all_gather x1, blocking collectives, local(): grads_all = lax.all_gather(out_grads, 'col', axis=0, tiled=True)  20 us
    dot_general x1, matrix products, local(): jnp.einsum('qkt,tk->qt', lifted, grad_rot.astype(jnp.float32), precision=...  19.9 us
    add x1, other arithmetic, local(): shifted = eigenvalues.astype(jnp.float32) + DAMPING  17 us
    all_gather x1, blocking collectives, local(): acts_all = lax.all_gather(in_acts, 'row', axis=0, tiled=True)  11 us
    all_gather x1, blocking collectives, local(): grad_rot = lax.all_gather(grad_mine, 'row', axis=0, tiled=True)  10.4 us
  transfers between devices with their start and end apart: 2, of which 0 were waited for; matrix products, arithmetic and copies ran while one was open for 42% of the time, Pallas kernels for 0%

profile of v1, /device:TPU:0, one launch (start us, length us, event | category | flops | bytes accessed | tf_op | source)
XLA Modules:
  0.0 204.7 jit_solution(4999511553947791724)
XLA Ops:
  7.4 0.0 all-gather.3.cloned.1.call-start
  7.4 11.0 %all_gather.17 = bf16[64,2048]{1,0:T(8,128)(2,1)S(1)} all-gather(bf16[8,2048]{1,0:T(8,128)(2,1)} %param.7), channel_id=1, replica_groups=mesh['row'=8,'col'=4] {'row'}, dimensions={0}, use_global_device_ids=true | all-gather | bytes 294912 | tf_op jit(solution)/shard_map/all_gather | solution.py:23
  18.3 3.7 %fusion.8 = f32[64,1024]{1,0:T(8,128)} fusion(bf16[64,2048]{1,0:T(8,128)(2,1)S(1)} %all_gather.17, bf16[2048,1024]{1,0:T(8,128)(2,1)} %param.9), kind=kOutput, calls=%fused_computation.10 | convolution fusion | flops 268435456 | bytes 4718592 | tf_op jit(solution)/shard_map/dot_general | solution.py:24
  22.1 0.0 all-gather.3.cloned.1.call-update
  22.1 0.0 reduce-scatter.2.cloned.1.call-start
  22.1 20.0 %all_gather.15 = bf16[64,3584]{1,0:T(8,128)(2,1)S(1)} all-gather(bf16[16,3584]{1,0:T(8,128)(2,1)} %param.6), channel_id=1, replica_groups=mesh['row'=8,'col'=4] {'col'}, dimensions={0}, use_global_device_ids=true | all-gather | bytes 573440 | tf_op jit(solution)/shard_map/all_gather | solution.py:15
  42.1 21.8 %fusion.7 = f32[64,7168]{1,0:T(8,128)} fusion(bf16[64,3584]{1,0:T(8,128)(2,1)S(1)} %all_gather.15, bf16[3584,7168]{1,0:T(8,128)(2,1)} %param.8), kind=kOutput, calls=%fused_computation.9 | convolution fusion | flops 3288334336 | bytes 53673984 | tf_op jit(solution)/shard_map/dot_general | solution.py:17
  64.0 0.0 reduce-scatter.2.cloned.1.call-update
  64.0 17.0 %convert_add_fusion = f32[7168,1024]{1,0:T(8,128)} fusion(bf16[7168,1024]{1,0:T(8,128)(2,1)} %param.10), kind=kLoop, calls=%fused_computation.3 | loop fusion | flops 14680064 | bytes 44040192 | tf_op jit(solution)/shard_map/add | solution.py:26
  81.0 0.0 all-gather.3.cloned.1.call-done
  81.0 1.3 reduce_sum.9
  82.3 45.7 %fusion = f32[2,7168,64]{1,2,0:T(8,128)} fusion(bf16[2,7168,1024]{2,1,0:T(8,128)(2,1)} %param.11, f32[7168,1024]{1,0:T(8,128)} %convert_add_fusion, bf16[64,1024]{1,0:T(8,128)(2,1)S(1)} %reduce_sum.9), kind=kOutput, calls=%fused_computation.1 | convolution fusion | flops 11303649280 | bytes 62521344 | tf_op jit(solution)/shard_map/qkj,tj->qkt/dot_general | solution.py:28
  128.0 0.0 reduce-scatter.2.cloned.1.call-done
  128.0 1.0 convert_element_type.14
  128.9 10.4 %all_gather.16 = bf16[64,7168]{1,0:T(8,128)(2,1)S(1)} all-gather(bf16[8,7168]{1,0:T(8,128)(2,1)S(1)} %convert_element_type.14), channel_id=1, replica_groups=mesh['row'=8,'col'=4] {'row'}, dimensions={0}, use_global_device_ids=true | all-gather | bytes 1032192 | tf_op jit(solution)/shard_map/all_gather | solution.py:22
  139.3 19.9 %fusion.2 = f32[64,1,2]{2,1,0:T(1,128)S(1)} fusion(f32[2,7168,64]{1,2,0:T(8,128)} %fusion, bf16[64,7168,1]{1,0,2:T(8,128)(2,1)S(1)} %bitcast.13), kind=kOutput, calls=%fused_computation.4 | convolution fusion | flops 11010048 | bytes 4588032 | tf_op jit(solution)/shard_map/qkt,tk->qt/dot_general | solution.py:35
  159.2 0.1 copy.9
  159.3 37.9 %psum.7 = f32[2,64]{1,0:T(2,128)} all-reduce(f32[2,64]{1,0:T(2,128)S(1)} %bitcast.14), channel_id=1, replica_groups=mesh['row'=8,'col'=4] {'row','col'}, use_global_device_ids=true, to_apply=%region_2.0 | all-reduce | flops 128 | bytes 1024 | tf_op jit(solution)/shard_map/psum | solution.py:38
Async XLA Ops:
  7.4 73.6 %all-gather.3.cloned.1.call-start = ((), (), s32[]{:S(2)}) async-start(), calls=%async_computation.2 | async-start | bytes 1310720 | tf_op jit(solution)/shard_map/all_gather | solution.py:10
  22.1 105.9 %reduce-scatter.2.cloned.1.call-start = ((), (), s32[]{:S(2)}) async-start(), calls=%async_computation.1 | async-start | bytes 2064384 | tf_op jit(solution)/shard_map/reduce_scatter | solution.py:16
Sparse Core Ops, SparseCore 0:
  22.2 31.5 all-gather.2
Sparse Core Ops, SparseCore 1:
  64.1 38.0 reduce-scatter.1

commit v2 on v0

--- a/solution.py
+++ b/solution.py
@@ -30,7 +30,7 @@
     partial_scores = jnp.einsum(
         "qkt,tk->qt", lifted, grad_rot.astype(jnp.float32), precision=lax.Precision.HIGHEST
     )
-    return lax.psum(partial_scores, ("row", "col"))
+    return jax.lax.psum(jax.lax.psum(partial_scores, "col"), "row")
 
 
 def solution(mesh):

time: 221 us -> 204 us (0.923)
  blocking collectives: 101 us -> 83.7 us
    psum x1 -> x2, blocking collectives: 37.8 us -> 20.7 us  [local(): return jax.lax.psum(jax.lax.psum(partial_scores, 'col'), 'row')]
  transfers between devices with their start and end apart: 1 -> 1, of which waited for: 0 -> 0; matrix products, arithmetic and copies ran while one was open for 29% -> 31% of each run, Pallas kernels for 0% -> 0%
where the time goes in v2:
time: 204 us
  matrix products  88 us (43%)
  blocking collectives  83.7 us (41%)
  other arithmetic  18.3 us (9%)
  between operations  13.4 us (7%)
    dot_general x1, matrix products, local(): jnp.einsum('qkj,tj->qkt', scaled, act_rot.astype(jnp.float32), precision=...  45.4 us
    psum x1, blocking collectives, local(): act_rot = lax.psum(act_part, 'col').astype(jnp.bfloat16)  25.6 us
    dot_general x1, matrix products, local(): jnp.dot(grads_all, out_basis, preferred_element_type=jnp.float32)  21.8 us
    psum x2, blocking collectives, local(): return jax.lax.psum(jax.lax.psum(partial_scores, 'col'), 'row')  20.7 us
    dot_general x1, matrix products, local(): jnp.einsum('qkt,tk->qt', lifted, grad_rot.astype(jnp.float32), precision=...  19.9 us
    add x1, other arithmetic, local(): shifted = eigenvalues.astype(jnp.float32) + DAMPING  17.4 us
    all_gather x1, blocking collectives, local(): grads_all = lax.all_gather(out_grads, 'col', axis=0, tiled=True)  17 us
    all_gather x1, blocking collectives, local(): grad_rot = lax.all_gather(grad_mine, 'row', axis=0, tiled=True)  11 us
  transfers between devices with their start and end apart: 1, of which 0 were waited for; matrix products, arithmetic and copies ran while one was open for 31% of the time, Pallas kernels for 0%

profile of v2, /device:TPU:0, one launch (start us, length us, event | category | flops | bytes accessed | tf_op | source)
XLA Modules:
  0.0 203.6 jit_solution(13734869235012368840)
XLA Ops:
  6.5 0.0 reduce-scatter.2.cloned.1.call-start
  6.5 17.0 %all_gather.9 = bf16[64,3584]{1,0:T(8,128)(2,1)S(1)} all-gather(bf16[16,3584]{1,0:T(8,128)(2,1)} %param.6), channel_id=1, replica_groups=mesh['row'=8,'col'=4] {'col'}, dimensions={0}, use_global_device_ids=true | all-gather | bytes 573440 | tf_op jit(solution)/shard_map/all_gather | solution.py:10
  23.5 21.8 %fusion.7 = f32[64,7168]{1,0:T(8,128)} fusion(bf16[64,3584]{1,0:T(8,128)(2,1)S(1)} %all_gather.9, bf16[3584,7168]{1,0:T(8,128)(2,1)} %param.8), kind=kOutput, calls=%fused_computation.9 | convolution fusion | flops 3288334336 | bytes 53673984 | tf_op jit(solution)/shard_map/dot_general | solution.py:12
  45.3 0.0 copy-start.1
  45.3 0.0 reduce-scatter.2.cloned.1.call-update
  45.4 0.0 copy-start
  45.4 17.4 %convert_add_fusion = f32[7168,1024]{1,0:T(8,128)} fusion(bf16[7168,1024]{1,0:T(8,128)(2,1)} %param.10), kind=kLoop, calls=%fused_computation.3 | loop fusion | flops 14680064 | bytes 44040192 | tf_op jit(solution)/shard_map/add | solution.py:21
  62.8 0.0 copy-done.1
  62.8 9.4 %all_gather.11 = bf16[64,2048]{1,0:T(8,128)(2,1)S(1)} all-gather(bf16[8,2048]{1,0:T(8,128)(2,1)S(1)} %copy-done.1), channel_id=1, replica_groups=mesh['row'=8,'col'=4] {'row'}, dimensions={0}, use_global_device_ids=true | all-gather | bytes 294912 | tf_op jit(solution)/shard_map/all_gather | solution.py:18
  72.2 0.0 copy-done
  72.2 0.8 fusion.8
  73.1 25.6 %all-reduce.1 = bf16[64,1024]{1,0:T(8,128)(2,1)S(1)} all-reduce(f32[64,1024]{1,0:T(8,128)S(1)} %fusion.8), channel_id=1, replica_groups=mesh['row'=8,'col'=4] {'col'}, use_global_device_ids=true, to_apply=%region_1.0 | all-reduce | flops 65536 | bytes 393216 | tf_op jit(solution)/shard_map/psum | solution.py:20
  98.7 45.4 %fusion = f32[2,7168,64]{1,2,0:T(8,128)} fusion(bf16[2,7168,1024]{2,1,0:T(8,128)(2,1)} %param.11, f32[7168,1024]{1,0:T(8,128)} %convert_add_fusion, bf16[64,1024]{1,0:T(8,128)(2,1)S(1)} %all-reduce.1), kind=kOutput, calls=%fused_computation.1 | convolution fusion | flops 11303649280 | bytes 62521344 | tf_op jit(solution)/shard_map/qkj,tj->qkt/dot_general | solution.py:23
  144.1 0.0 reduce-scatter.2.cloned.1.call-done
  144.1 1.0 convert_element_type.14
  145.1 11.0 %all_gather.10 = bf16[64,7168]{1,0:T(8,128)(2,1)S(1)} all-gather(bf16[8,7168]{1,0:T(8,128)(2,1)S(1)} %convert_element_type.14), channel_id=1, replica_groups=mesh['row'=8,'col'=4] {'row'}, dimensions={0}, use_global_device_ids=true | all-gather | bytes 1032192 | tf_op jit(solution)/shard_map/all_gather | solution.py:17
  156.0 19.9 %fusion.2 = f32[64,1,2]{2,1,0:T(1,128)S(1)} fusion(f32[2,7168,64]{1,2,0:T(8,128)} %fusion, bf16[64,7168,1]{1,0,2:T(8,128)(2,1)S(1)} %bitcast.11), kind=kOutput, calls=%fused_computation.4 | convolution fusion | flops 11010048 | bytes 4588032 | tf_op jit(solution)/shard_map/qkt,tk->qt/dot_general | solution.py:30
  175.9 0.1 copy.9
  176.0 8.4 %psum.22 = f32[2,64]{1,0:T(2,128)S(1)} all-reduce(f32[2,64]{1,0:T(2,128)S(1)} %bitcast.12), channel_id=1, replica_groups=mesh['row'=8,'col'=4] {'col'}, use_global_device_ids=true, to_apply=%region_2.0 | all-reduce | flops 128 | bytes 1024 | tf_op jit(solution)/shard_map/psum | solution.py:33
  184.4 12.3 %psum.23 = f32[2,64]{1,0:T(2,128)} all-reduce(f32[2,64]{1,0:T(2,128)S(1)} %psum.22), channel_id=1, replica_groups=mesh['row'=8,'col'=4] {'row'}, use_global_device_ids=true, to_apply=%region_3.0 | all-reduce | flops 128 | bytes 1024 | tf_op jit(solution)/shard_map/psum | solution.py:33
Async XLA Ops:
  6.5 137.6 %reduce-scatter.2.cloned.1.call-start = ((), (), s32[]{:S(2)}) async-start(), calls=%async_computation.1 | async-start | bytes 2064384 | tf_op jit(solution)/shard_map/reduce_scatter | solution.py:11
  45.3 17.4 %copy-start.1 = (bf16[8,2048]{1,0:T(8,128)(2,1)S(1)}, bf16[8,2048]{1,0:T(8,128)(2,1)}, u32[]{:S(2)}) copy-start(bf16[8,2048]{1,0:T(8,128)(2,1)} %param.7) | copy-start | bytes 98308
  45.4 26.8 %copy-start = (bf16[2048,1024]{1,0:T(8,128)(2,1)S(1)}, bf16[2048,1024]{1,0:T(8,128)(2,1)}, u32[]{:S(2)}) copy-start(bf16[2048,1024]{1,0:T(8,128)(2,1)} %param.9) | copy-start | bytes 12582916
Sparse Core Ops, SparseCore 0:
  45.5 42.0 reduce-scatter.1
